TPU v7x, 32 devices: a whole 2x2x4 slice. The times are simulated.
32 devices in a mesh: grp: 2 (over y), cell: 8 (over z, x), gene: 2 (over core).
Axes of the slice: x: 2, y: 2, z: 4, core: 2. Of those that a mesh axis runs over, the one named last changes fastest.
Arguments:
- expression: bfloat16 [2048, 16384], P(('grp', 'cell'), 'gene'), parts along dimension 0, may hold values from -6 to 6
- design: bfloat16 [2048, 128], P(('grp', 'cell')), parts along dimension 0, may hold values from -24 to 24
- quantile_level: float32 [16384], P('gene'), may hold values from 0.1 to 0.9
Outputs:
- quantile_slack: bfloat16 [2048, 16384], P(('grp', 'cell'), 'gene'), parts along dimension 0
- low_rank_coef: float32 [32768, 128], P(('grp', 'gene', 'cell')), parts along dimension 0
There are 2 independent parts, one for each index of `grp`. A program takes and returns all parts, laid end to end along the dimension named above; an argument that names none is the same for every part. Nothing has to cross between parts.
All inputs are finite; a program needn't handle non-finite values.
Results may differ from a plain program's by a relative error of at most 0.0025.
The roundings to bfloat16 on the way count: a program that leaves them out, or rounds other values in their place, can miss the bound.
Values may be sent and summed in bfloat16 or wider, within the bound.
No kernel may reach another device: no remote copies, remote signals or barrier semaphores. Data moves between devices by JAX's collectives and lax.ppermute only.
A program may use at most 64 MiB of HBM per device.

v0:
```python
import functools
import math
import jax
import jax.numpy as jnp
from jax import lax
from jax.sharding import PartitionSpec as P

NS_STEPS = 8
shrink_rate = 0.25


def matmul(left, right):
    return jnp.dot(left, right, precision=lax.Precision.HIGHEST)


def invert(matrix):
    identity = jnp.eye(matrix.shape[0], dtype=jnp.float32)
    factor = jnp.linalg.cholesky(matrix)
    lower_inv = lax.linalg.triangular_solve(factor, identity, left_side=True, lower=True)
    return matmul(lower_inv.T, lower_inv)


def newton(moment):
    identity = jnp.eye(moment.shape[0], dtype=jnp.float32)
    current = moment / jnp.trace(moment)
    root_inv = identity
    for sweep in range(NS_STEPS):
        middle = 1.5 * identity - 0.5 * matmul(root_inv, current)
        current = matmul(current, middle)
        root_inv = matmul(middle, root_inv)
    return root_inv


def cell_ring(mesh):
    devices = mesh.devices
    names = list(mesh.axis_names)
    index = [0] * len(names)
    index[names.index("cell")] = slice(None)
    line = list(devices[tuple(index)].reshape(-1))
    n = len(line)
    try:
        coords = [tuple(d.coords) for d in line]
    except (AttributeError, TypeError):
        return list(range(n))
    varying = [a for a in range(len(coords[0])) if len({c[a] for c in coords}) > 1]
    where = {c: i for i, c in enumerate(coords)}
    if len(varying) == 1:
        return sorted(range(n), key=lambda i: coords[i][varying[0]])
    if len(varying) != 2:
        return list(range(n))
    sizes = [len({c[a] for c in coords}) for a in varying]
    if sizes[0] * sizes[1] != n:
        return list(range(n))
    if sizes[0] % 2:
        varying, sizes = (varying[::-1], sizes[::-1])
        if sizes[0] % 2:
            return list(range(n))
    lows = [min((c[a] for c in coords)) for a in varying]
    path = []
    for u in range(sizes[0]):
        span = range(1, sizes[1]) if u % 2 == 0 else range(sizes[1] - 1, 0, -1)
        path += [(u, v) for v in span]
    path += [(u, 0) for u in range(sizes[0] - 1, -1, -1)]
    order = []
    for u, v in path:
        key = list(coords[0])
        key[varying[0]] = lows[0] + u
        key[varying[1]] = lows[1] + v
        order.append(where[tuple(key)])
    return order


def gather_blocks(block, axis):
    n = lax.axis_size(axis)
    me = lax.axis_index(axis)
    received = [block]
    for shift in range(1, n):
        pairs = [(i, (i + shift) % n) for i in range(n)]
        received.append(lax.ppermute(block, axis, pairs))
    stacked = jnp.stack(received)
    return jnp.take(stacked, (me - jnp.arange(n)) % n, axis=0)


def butterfly_sum(value, axis):
    n = lax.axis_size(axis)
    if n & n - 1:
        return lax.psum(value, axis)
    bit = 1
    while bit < n:
        pairs = [(i, i ^ bit) for i in range(n)]
        value = value + lax.ppermute(value, axis, pairs)
        bit *= 2
    return value


def per_device(ring, expression, design, quantile_level):
    n = len(ring)
    width = design.shape[1]
    span = expression.shape[1] // n
    identity = jnp.eye(width, dtype=jnp.float32)
    design_all = gather_blocks(design, "cell").reshape(-1, width)
    sent = expression + (design_all[0, 0] * 0).astype(expression.dtype)
    expression_genes = lax.all_to_all(sent, "cell", 1, 0, tiled=True)
    gram_total = lax.dot_general(
        design_all, design_all, (((0,), (0,)), ((), ())), preferred_element_type=jnp.float32
    )
    inverse = invert(gram_total + identity)
    crossed = lax.dot_general(
        expression_genes, design_all, (((0,), (0,)), ((), ())), preferred_element_type=jnp.float32
    )
    coef = matmul(crossed, inverse)
    local_moment = lax.dot_general(
        coef, coef, (((0,), (0,)), ((), ())), precision=lax.Precision.HIGHEST
    )
    chip_moment = butterfly_sum(local_moment, "gene")
    moment = jnp.sum(gather_blocks(chip_moment, "cell"), axis=0)
    root_inv = newton(moment)
    low_rank_coef = coef - shrink_rate / math.sqrt(width) * matmul(coef, root_inv)
    coef_low_t = coef.astype(jnp.bfloat16).T
    ring_arr = jnp.array(ring, dtype=jnp.int32)
    pos_arr = jnp.array([ring.index(i) for i in range(n)], dtype=jnp.int32)
    me = lax.axis_index("cell")
    pos = pos_arr[me]
    forward = [(ring[q], ring[(q + 1) % n]) for q in range(n)]
    backward = [(ring[(q + 1) % n], ring[q]) for q in range(n)]
    out = jnp.zeros(expression.shape, jnp.bfloat16)

    def place(out, block, owner):
        start = owner * span
        fitted = jnp.dot(design, block, preferred_element_type=jnp.float32)
        local = lax.dynamic_slice_in_dim(expression, start, span, axis=1).astype(jnp.float32)
        level = lax.dynamic_slice_in_dim(quantile_level, start, span)[None, :]
        slack = local - fitted
        piece = (slack - jnp.clip(slack, level - 1.0, level)).astype(jnp.bfloat16)
        return lax.dynamic_update_slice_in_dim(out, piece, start, axis=1)

    out = place(out, coef_low_t, me)
    ahead, behind = (coef_low_t, coef_low_t)
    for step in range(1, n // 2 + 1):
        ahead = lax.ppermute(ahead, "cell", forward)
        out = place(out, ahead, ring_arr[(pos - step) % n])
        if step <= (n - 1) // 2:
            behind = lax.ppermute(behind, "cell", backward)
            out = place(out, behind, ring_arr[(pos + step) % n])
    return (out, low_rank_coef)


def solution(mesh):
    placed = (P(("grp", "cell"), "gene"), P(("grp", "cell"), None), P("gene"))
    ring = cell_ring(mesh)
    return jax.shard_map(
        functools.partial(per_device, ring),
        mesh=mesh,
        in_specs=placed,
        out_specs=(P(("grp", "cell"), "gene"), P(("grp", "gene", "cell"), None)),
        check_vma=False,
    )
```

profile of v0, /device:TPU:0, one launch (start us, length us, event | category | flops | bytes accessed | tf_op | source)
XLA Modules:
  0.0 163.7 jit_solution(11076976861056799472)
XLA Ops:
  0.6 6.1 %collective-permute-start.6 = (bf16[128,128]{1,0:T(8,128)(2,1)}, bf16[128,128]{1,0:T(8,128)(2,1)S(1)}, u32[]{:S(2)}, u32[]{:S(2)}) collective-permute-start(bf16[128,128]{1,0:T(8,128)(2,1)} %param.6), channel_id=1, source_target_pairs={{0,14},{2,0},{4,2},{6,4},{8,6},{10,8},{12,10},{14,12},{1,15},{3,1}... | collective-permute-start | bytes 98312 | tf_op jit(solution)/shard_map/ppermute | solution.py:79
  7.1 3.0 %collective-permute-start.3 = (bf16[128,128]{1,0:T(8,128)(2,1)}, bf16[128,128]{1,0:T(8,128)(2,1)S(1)}, u32[]{:S(2)}, u32[]{:S(2)}) collective-permute-start(bf16[128,128]{1,0:T(8,128)(2,1)} %param.6), channel_id=1, source_target_pairs={{0,8},{2,10},{4,12},{6,14},{8,0},{10,2},{12,4},{14,6},{1,9},{3,11}... | collective-permute-start | bytes 98312 | tf_op jit(solution)/shard_map/ppermute | solution.py:79
  10.1 1.5 collective-permute-start
  11.7 0.8 constant_dynamic-update-slice_fusion.7
  13.1 3.2 %copy.43 = bf16[128,8192]{0,1:T(8,128)(2,1)S(1)} copy(bf16[128,8192]{1,0:T(8,128)(2,1)} %param.5) | data formatting | bytes 4194304 | tf_op args[0]
  16.3 0.7 collective-permute-done
  17.0 5.7 %collective-permute-done.1 = bf16[128,128]{1,0:T(8,128)(2,1)S(1)} collective-permute-done((bf16[128,128]{1,0:T(8,128)(2,1)S(1)}, bf16[128,128]{1,0:T(8,128)(2,1)S(1)}, u32[]{:S(2)}, u32[]{:S(2)}) %collective-permute-start.1) | collective-permute-done | bytes 32800 | tf_op jit(solution)/shard_map/ppermute | solution.py:79
  22.7 5.7 %collective-permute-done.2 = bf16[128,128]{1,0:T(8,128)(2,1)S(1)} collective-permute-done((bf16[128,128]{1,0:T(8,128)(2,1)S(1)}, bf16[128,128]{1,0:T(8,128)(2,1)S(1)}, u32[]{:S(2)}, u32[]{:S(2)}) %collective-permute-start.2) | collective-permute-done | bytes 32800 | tf_op jit(solution)/shard_map/ppermute | solution.py:79
  30.9 1.5 broadcast_add_fusion
  32.4 3.9 %copy.45 = bf16[128,8,1024]{2,0,1:T(8,128)(2,1)} copy(bf16[128,8,1024]{0,2,1:T(8,128)(2,1)} %bitcast.190) | data formatting | bytes 4194304 | tf_op jit(solution)/shard_map/all_to_all | solution.py:103
  36.3 4.5 %all-to-all-start = ((bf16[128,8,1024]{2,0,1:T(8,128)(2,1)}), bf16[128,8,1024]{2,0,1:T(8,128)(2,1)}, u32[]{:S(2)}, u32[]{:S(2)}) async-start(bf16[128,8,1024]{2,0,1:T(8,128)(2,1)} %copy.45), calls=%async_computation | async-start | bytes 4194304 | tf_op jit(solution)/shard_map/all_to_all | solution.py:103
  46.1 0.7 fusion.35
  51.3 0.6 broadcast_add_fusion.1
  52.4 11.7 %cholesky.29 = f32[128,128]{1,0:T(8,128)S(1)} custom-call(f32[128,128]{1,0:T(8,128)S(1)} %fusion.27), custom_call_target="Cholesky" | custom-call | tf_op jit(solution)/shard_map/jit(cholesky)/cholesky | solution.py:18
  64.2 0.6 compare_reduce_fusion
  64.8 0.7 fusion.23
  65.5 9.8 %custom-call.6 = f32[1,128,128]{1,2,0:T(8,128)S(1)} custom-call(f32[1,128,128]{2,1,0:T(8,128)S(1)} %fusion.23), custom_call_target="InvertDiagBlocksLowerTriangular" | custom-call | tf_op jit(solution)/shard_map/triangular_solve | solution.py:19
  75.8 9.4 %all-to-all-done = bf16[128,8,1024]{2,0,1:T(8,128)(2,1)} async-done(((bf16[128,8,1024]{2,0,1:T(8,128)(2,1)}), bf16[128,8,1024]{2,0,1:T(8,128)(2,1)}, u32[]{:S(2)}, u32[]{:S(2)}) %all-to-all-start) | async-done | bytes 2097184 | tf_op jit(solution)/shard_map/all_to_all | solution.py:103
  85.2 3.9 %copy.46 = bf16[128,8,1024]{0,2,1:T(8,128)(2,1)} copy(bf16[128,8,1024]{2,0,1:T(8,128)(2,1)} %all-to-all-done) | data formatting | bytes 4194304 | tf_op jit(solution)/shard_map/all_to_all | solution.py:103
  89.1 2.4 %fusion.2 = f32[1024,128]{1,0:T(8,128)S(1)} fusion(bf16[128,8,1024]{0,2,1:T(8,128)(2,1)} %copy.46, bf16[8,128,128]{2,1,0:T(8,128)(2,1)S(1)} %gather_fusion, pred[8]{0:T(512)(128)(4,1)S(1)} %compare_and_fusion), kind=kOutput, calls=%fused_computation.4 | convolution fusion | flops 268566528 | bytes 2883592 | tf_op jit(solution)/shard_map/dot_general | solution.py:108
  92.1 1.0 fusion.38
  93.1 1.3 collective-permute-start.8
  94.4 0.8 collective-permute-start.7
  95.7 0.9 collective-permute-done.14
  96.6 1.5 bitcast_dynamic-update-slice_fusion.7
  98.1 1.3 collective-permute-start.15
  99.3 1.5 broadcast_in_dim.41
  100.9 0.7 constant_dynamic-update-slice_fusion.15
  101.6 1.4 collective-permute-start.20
  103.6 1.4 collective-permute-done.15
  105.6 0.6 bitcast_dynamic-update-slice_fusion.6
  106.2 4.9 %collective-permute-done.16 = f32[128,128]{1,0:T(8,128)S(1)} collective-permute-done((f32[128,128]{1,0:T(8,128)S(1)}, f32[128,128]{1,0:T(8,128)S(1)}, u32[]{:S(2)}, u32[]{:S(2)}) %collective-permute-start.16) | collective-permute-done | bytes 65568 | tf_op jit(solution)/shard_map/ppermute | solution.py:79
  111.1 0.7 collective-permute-start.17
  111.8 0.6 bitcast_dynamic-update-slice_fusion.5
  112.4 4.8 %collective-permute-done.17 = f32[128,128]{1,0:T(8,128)S(1)} collective-permute-done((f32[128,128]{1,0:T(8,128)S(1)}, f32[128,128]{1,0:T(8,128)S(1)}, u32[]{:S(2)}, u32[]{:S(2)}) %collective-permute-start.17) | collective-permute-done | bytes 65568 | tf_op jit(solution)/shard_map/ppermute | solution.py:79
  117.2 1.2 collective-permute-start.18
  118.4 0.6 bitcast_dynamic-update-slice_fusion.4
  119.0 3.5 %collective-permute-done.18 = f32[128,128]{1,0:T(8,128)S(1)} collective-permute-done((f32[128,128]{1,0:T(8,128)S(1)}, f32[128,128]{1,0:T(8,128)S(1)}, u32[]{:S(2)}, u32[]{:S(2)}) %collective-permute-start.18) | collective-permute-done | bytes 65568 | tf_op jit(solution)/shard_map/ppermute | solution.py:79
  123.2 0.6 bitcast_dynamic-update-slice_fusion.2
  123.9 0.6 bitcast_dynamic-update-slice_fusion.1
  124.5 2.3 %collective-permute-done.21 = f32[128,128]{1,0:T(8,128)S(1)} collective-permute-done((f32[128,128]{1,0:T(8,128)S(1)}, f32[128,128]{1,0:T(8,128)S(1)}, u32[]{:S(2)}, u32[]{:S(2)}) %collective-permute-start.21) | collective-permute-done | bytes 65568 | tf_op jit(solution)/shard_map/ppermute | solution.py:79
  126.8 0.6 bitcast_dynamic-update-slice_fusion
  127.5 1.6 gather_fusion.1
  129.1 0.8 select_reduce_fusion
  130.5 0.8 fusion.21
  131.3 0.8 fusion.29
  136.6 1.4 fusion.13
  138.4 1.3 subtract_convert_fusion.6
  139.7 1.3 subtract_convert_fusion.5
  141.3 1.8 %collective-permute-start.10 = (bf16[128,1024]{0,1:T(8,128)(2,1)}, bf16[128,1024]{0,1:T(8,128)(2,1)S(1)}, u32[]{:S(2)}, u32[]{:S(2)}) collective-permute-start(bf16[128,1024]{0,1:T(8,128)(2,1)} %collective-permute-done.8), channel_id=1, source_target_pairs={{8,4},{12,8},{14,12},{10,14},{6,10},{2,6},{0,2},{4,0},{9,5},{13,9}... | collective-permute-start | bytes 786440 | tf_op jit(solution)/shard_map/ppermute | solution.py:143
  143.2 0.7 constant_dynamic-update-slice_fusion.14
  143.9 0.7 constant_dynamic-update-slice_fusion.13
  144.6 2.3 %collective-permute-done.9 = bf16[128,1024]{0,1:T(8,128)(2,1)S(1)} collective-permute-done((bf16[128,1024]{0,1:T(8,128)(2,1)}, bf16[128,1024]{0,1:T(8,128)(2,1)S(1)}, u32[]{:S(2)}, u32[]{:S(2)}) %collective-permute-start.9) | collective-permute-done | bytes 262176 | tf_op jit(solution)/shard_map/ppermute | solution.py:140
  147.5 1.5 collective-permute-done.10
  149.0 0.7 copy-done.7
  150.4 1.9 %collective-permute-start.12 = (bf16[128,1024]{0,1:T(8,128)(2,1)}, bf16[128,1024]{0,1:T(8,128)(2,1)S(1)}, u32[]{:S(2)}, u32[]{:S(2)}) collective-permute-start(bf16[128,1024]{0,1:T(8,128)(2,1)} %copy-done.7), channel_id=1, source_target_pairs={{8,4},{12,8},{14,12},{10,14},{6,10},{2,6},{0,2},{4,0},{9,5},{13,9}... | collective-permute-start | bytes 786440 | tf_op jit(solution)/shard_map/ppermute | solution.py:143
  152.3 0.7 constant_dynamic-update-slice_fusion.12
  153.0 0.7 constant_dynamic-update-slice_fusion.11
  153.7 2.4 %collective-permute-done.11 = bf16[128,1024]{0,1:T(8,128)(2,1)S(1)} collective-permute-done((bf16[128,1024]{0,1:T(8,128)(2,1)S(1)}, bf16[128,1024]{0,1:T(8,128)(2,1)S(1)}, u32[]{:S(2)}, u32[]{:S(2)}) %collective-permute-start.11) | collective-permute-done | bytes 262176 | tf_op jit(solution)/shard_map/ppermute | solution.py:140
  156.5 0.7 collective-permute-done.12
  157.8 0.7 constant_dynamic-update-slice_fusion.10
  158.6 0.7 constant_dynamic-update-slice_fusion.9
  159.3 3.2 %collective-permute-done.13 = bf16[128,1024]{0,1:T(8,128)(2,1)S(1)} collective-permute-done((bf16[128,1024]{0,1:T(8,128)(2,1)S(1)}, bf16[128,1024]{0,1:T(8,128)(2,1)S(1)}, u32[]{:S(2)}, u32[]{:S(2)}) %collective-permute-start.13) | collective-permute-done | bytes 262176 | tf_op jit(solution)/shard_map/ppermute | solution.py:140
  163.0 0.7 constant_dynamic-update-slice_fusion.8
  (96 shorter events, 15.1 us)
Async XLA Ops:
  0.6 27.9 %collective-permute-start.6 = (bf16[128,128]{1,0:T(8,128)(2,1)}, bf16[128,128]{1,0:T(8,128)(2,1)S(1)}, u32[]{:S(2)}, u32[]{:S(2)}) collective-permute-start(bf16[128,128]{1,0:T(8,128)(2,1)} %param.6), channel_id=1, source_target_pairs={{0,14},{2,0},{4,2},{6,4},{8,6},{10,8},{12,10},{14,12},{1,15},{3,1}... | collective-permute-start | bytes 98312 | tf_op jit(solution)/shard_map/ppermute | solution.py:79
  6.7 21.8 %collective-permute-start.5 = (bf16[128,128]{1,0:T(8,128)(2,1)}, bf16[128,128]{1,0:T(8,128)(2,1)S(1)}, u32[]{:S(2)}, u32[]{:S(2)}) collective-permute-start(bf16[128,128]{1,0:T(8,128)(2,1)} %param.6), channel_id=1, source_target_pairs={{0,12},{2,14},{4,0},{6,2},{8,4},{10,6},{12,8},{14,10},{1,13},{3,15... | collective-permute-start | bytes 98312 | tf_op jit(solution)/shard_map/ppermute | solution.py:79
  7.1 21.3 %collective-permute-start.4 = (bf16[128,128]{1,0:T(8,128)(2,1)}, bf16[128,128]{1,0:T(8,128)(2,1)S(1)}, u32[]{:S(2)}, u32[]{:S(2)}) collective-permute-start(bf16[128,128]{1,0:T(8,128)(2,1)} %param.6), channel_id=1, source_target_pairs={{0,10},{2,12},{4,14},{6,0},{8,2},{10,4},{12,6},{14,8},{1,11},{3,13... | collective-permute-start | bytes 98312 | tf_op jit(solution)/shard_map/ppermute | solution.py:79
  7.1 21.3 %collective-permute-start.3 = (bf16[128,128]{1,0:T(8,128)(2,1)}, bf16[128,128]{1,0:T(8,128)(2,1)S(1)}, u32[]{:S(2)}, u32[]{:S(2)}) collective-permute-start(bf16[128,128]{1,0:T(8,128)(2,1)} %param.6), channel_id=1, source_target_pairs={{0,8},{2,10},{4,12},{6,14},{8,0},{10,2},{12,4},{14,6},{1,9},{3,11}... | collective-permute-start | bytes 98312 | tf_op jit(solution)/shard_map/ppermute | solution.py:79
  10.1 6.8 %collective-permute-start = (bf16[128,128]{1,0:T(8,128)(2,1)}, bf16[128,128]{1,0:T(8,128)(2,1)S(1)}, u32[]{:S(2)}, u32[]{:S(2)}) collective-permute-start(bf16[128,128]{1,0:T(8,128)(2,1)} %param.6), channel_id=1, source_target_pairs={{0,2},{2,4},{4,6},{6,8},{8,10},{10,12},{12,14},{14,0},{1,3},{3,5},... | collective-permute-start | bytes 98312 | tf_op jit(solution)/shard_map/ppermute | solution.py:79
  11.7 77.5 %copy-start.6 = (pred[8]{0:T(512)(128)(4,1)}, pred[8]{0:T(512)(128)(4,1)S(1)}, u32[]{:S(2)}) copy-start(pred[8]{0:T(512)(128)(4,1)S(1)} %compare_and_fusion) | copy-start | bytes 28
  13.1 3.9 %copy-start = (bf16[128,128]{1,0:T(8,128)(2,1)S(1)}, bf16[128,128]{1,0:T(8,128)(2,1)}, u32[]{:S(2)}) copy-start(bf16[128,128]{1,0:T(8,128)(2,1)} %param.6) | copy-start | bytes 98308
  17.0 5.7 %collective-permute-start.1 = (bf16[128,128]{1,0:T(8,128)(2,1)S(1)}, bf16[128,128]{1,0:T(8,128)(2,1)S(1)}, u32[]{:S(2)}, u32[]{:S(2)}) collective-permute-start(bf16[128,128]{1,0:T(8,128)(2,1)S(1)} %copy-done), channel_id=1, source_target_pairs={{0,4},{2,6},{4,8},{6,10},{8,12},{10,14},{12,0},{14,2},{1,5},{3,7},... | collective-permute-start | bytes 98312 | tf_op jit(solution)/shard_map/ppermute | solution.py:79
  22.7 5.7 %collective-permute-start.2 = (bf16[128,128]{1,0:T(8,128)(2,1)S(1)}, bf16[128,128]{1,0:T(8,128)(2,1)S(1)}, u32[]{:S(2)}, u32[]{:S(2)}) collective-permute-start(bf16[128,128]{1,0:T(8,128)(2,1)S(1)} %copy-done), channel_id=1, source_target_pairs={{0,6},{2,8},{4,10},{6,12},{8,14},{10,0},{12,2},{14,4},{1,7},{3,9},... | collective-permute-start | bytes 98312 | tf_op jit(solution)/shard_map/ppermute | solution.py:79
  36.3 4.5 %copy-start.8 = (s32[8]{0:T(128)S(1)}, s32[8]{0:T(128)}, u32[]{:S(2)}) copy-start(s32[8]{0:T(128)} %constant.188.clone) | copy-start | bytes 100
  36.3 9.8 %copy-start.2 = (s32[8]{0:T(128)S(1)}, s32[8]{0:T(128)}, u32[]{:S(2)}) copy-start(s32[8]{0:T(128)} %constant.187.clone) | copy-start | bytes 100
  36.3 15.0 %copy-start.1 = (f32[8192]{0:T(1024)S(1)}, f32[8192]{0:T(1024)}, u32[]{:S(2)}) copy-start(f32[8192]{0:T(1024)} %param.7) | copy-start | bytes 98308
  36.3 48.9 %all-to-all-start = ((bf16[128,8,1024]{2,0,1:T(8,128)(2,1)}), bf16[128,8,1024]{2,0,1:T(8,128)(2,1)}, u32[]{:S(2)}, u32[]{:S(2)}) async-start(bf16[128,8,1024]{2,0,1:T(8,128)(2,1)} %copy.45), calls=%async_computation | async-start | bytes 4194304 | tf_op jit(solution)/shard_map/all_to_all | solution.py:103
  93.1 46.6 %collective-permute-start.8 = (bf16[128,1024]{0,1:T(8,128)(2,1)S(1)}, bf16[128,1024]{0,1:T(8,128)(2,1)}, u32[]{:S(2)}, u32[]{:S(2)}) collective-permute-start(bf16[128,1024]{0,1:T(8,128)(2,1)S(1)} %convert_bitcast_fusion), channel_id=1, source_target_pairs={{8,4},{12,8},{14,12},{10,14},{6,10},{2,6},{0,2},{4,0},{9,5},{13,9}... | collective-permute-start | bytes 786440 | tf_op jit(solution)/shard_map/ppermute | solution.py:143
  94.4 43.6 %collective-permute-start.7 = (bf16[128,1024]{0,1:T(8,128)(2,1)S(1)}, bf16[128,1024]{0,1:T(8,128)(2,1)}, u32[]{:S(2)}, u32[]{:S(2)}) collective-permute-start(bf16[128,1024]{0,1:T(8,128)(2,1)S(1)} %convert_bitcast_fusion), channel_id=1, source_target_pairs={{4,8},{8,12},{12,14},{14,10},{10,6},{6,2},{2,0},{0,4},{5,9},{9,13}... | collective-permute-start | bytes 786440 | tf_op jit(solution)/shard_map/ppermute | solution.py:140
  95.2 1.4 collective-permute-start.14
  98.1 7.0 %collective-permute-start.15 = (f32[128,128]{1,0:T(8,128)S(1)}, f32[128,128]{1,0:T(8,128)S(1)}, u32[]{:S(2)}, u32[]{:S(2)}) collective-permute-start(f32[128,128]{1,0:T(8,128)S(1)} %get-tuple-element.3), channel_id=1, source_target_pairs={{0,2},{2,4},{4,6},{6,8},{8,10},{10,12},{12,14},{14,0},{1,3},{3,5},... | collective-permute-start | bytes 196616 | tf_op jit(solution)/shard_map/ppermute | solution.py:79
  101.6 22.3 %collective-permute-start.20 = (f32[128,128]{1,0:T(8,128)S(1)}, f32[128,128]{1,0:T(8,128)S(1)}, u32[]{:S(2)}, u32[]{:S(2)}) collective-permute-start(f32[128,128]{1,0:T(8,128)S(1)} %get-tuple-element.3), channel_id=1, source_target_pairs={{0,12},{2,14},{4,0},{6,2},{8,4},{10,6},{12,8},{14,10},{1,13},{3,15... | collective-permute-start | bytes 196616 | tf_op jit(solution)/shard_map/ppermute | solution.py:79
  103.0 20.2 %collective-permute-start.19 = (f32[128,128]{1,0:T(8,128)S(1)}, f32[128,128]{1,0:T(8,128)S(1)}, u32[]{:S(2)}, u32[]{:S(2)}) collective-permute-start(f32[128,128]{1,0:T(8,128)S(1)} %get-tuple-element.3), channel_id=1, source_target_pairs={{0,10},{2,12},{4,14},{6,0},{8,2},{10,4},{12,6},{14,8},{1,11},{3,13... | collective-permute-start | bytes 196616 | tf_op jit(solution)/shard_map/ppermute | solution.py:79
  105.0 6.1 %collective-permute-start.16 = (f32[128,128]{1,0:T(8,128)S(1)}, f32[128,128]{1,0:T(8,128)S(1)}, u32[]{:S(2)}, u32[]{:S(2)}) collective-permute-start(f32[128,128]{1,0:T(8,128)S(1)} %get-tuple-element.3), channel_id=1, source_target_pairs={{0,4},{2,6},{4,8},{6,10},{8,12},{10,14},{12,0},{14,2},{1,5},{3,7},... | collective-permute-start | bytes 196616 | tf_op jit(solution)/shard_map/ppermute | solution.py:79
  111.1 6.1 %collective-permute-start.17 = (f32[128,128]{1,0:T(8,128)S(1)}, f32[128,128]{1,0:T(8,128)S(1)}, u32[]{:S(2)}, u32[]{:S(2)}) collective-permute-start(f32[128,128]{1,0:T(8,128)S(1)} %get-tuple-element.3), channel_id=1, source_target_pairs={{0,6},{2,8},{4,10},{6,12},{8,14},{10,0},{12,2},{14,4},{1,7},{3,9},... | collective-permute-start | bytes 196616 | tf_op jit(solution)/shard_map/ppermute | solution.py:79
  117.2 5.4 %collective-permute-start.18 = (f32[128,128]{1,0:T(8,128)S(1)}, f32[128,128]{1,0:T(8,128)S(1)}, u32[]{:S(2)}, u32[]{:S(2)}) collective-permute-start(f32[128,128]{1,0:T(8,128)S(1)} %get-tuple-element.3), channel_id=1, source_target_pairs={{0,8},{2,10},{4,12},{6,14},{8,0},{10,2},{12,4},{14,6},{1,9},{3,11}... | collective-permute-start | bytes 196616 | tf_op jit(solution)/shard_map/ppermute | solution.py:79
  122.6 4.3 %collective-permute-start.21 = (f32[128,128]{1,0:T(8,128)S(1)}, f32[128,128]{1,0:T(8,128)S(1)}, u32[]{:S(2)}, u32[]{:S(2)}) collective-permute-start(f32[128,128]{1,0:T(8,128)S(1)} %get-tuple-element.3), channel_id=1, source_target_pairs={{0,14},{2,0},{4,2},{6,4},{8,6},{10,8},{12,10},{14,12},{1,15},{3,1}... | collective-permute-start | bytes 196616 | tf_op jit(solution)/shard_map/ppermute | solution.py:79
  133.2 5.1 %copy-start.4 = (f32[1024]{0:T(1024)S(1)}, f32[1024]{0:T(1024)}, u32[]{:S(2)}) copy-start(f32[1024]{0:T(1024)} %get-tuple-element.28) | copy-start | bytes 12292
  133.2 5.1 %copy-start.5 = (f32[1024]{0:T(1024)S(1)}, f32[1024]{0:T(1024)}, u32[]{:S(2)}) copy-start(f32[1024]{0:T(1024)} %get-tuple-element.29) | copy-start | bytes 12292
  134.3 5.4 %copy-start.3 = (f32[1024]{0:T(1024)S(1)}, f32[1024]{0:T(1024)}, u32[]{:S(2)}) copy-start(f32[1024]{0:T(1024)} %get-tuple-element.27) | copy-start | bytes 12292
  138.0 8.9 %collective-permute-start.9 = (bf16[128,1024]{0,1:T(8,128)(2,1)}, bf16[128,1024]{0,1:T(8,128)(2,1)S(1)}, u32[]{:S(2)}, u32[]{:S(2)}) collective-permute-start(bf16[128,1024]{0,1:T(8,128)(2,1)} %collective-permute-done.7), channel_id=1, source_target_pairs={{4,8},{8,12},{12,14},{14,10},{10,6},{6,2},{2,0},{0,4},{5,9},{9,13}... | collective-permute-start | bytes 786440 | tf_op jit(solution)/shard_map/ppermute | solution.py:140
  141.3 7.7 %collective-permute-start.10 = (bf16[128,1024]{0,1:T(8,128)(2,1)}, bf16[128,1024]{0,1:T(8,128)(2,1)S(1)}, u32[]{:S(2)}, u32[]{:S(2)}) collective-permute-start(bf16[128,1024]{0,1:T(8,128)(2,1)} %collective-permute-done.8), channel_id=1, source_target_pairs={{8,4},{12,8},{14,12},{10,14},{6,10},{2,6},{0,2},{4,0},{9,5},{13,9}... | collective-permute-start | bytes 786440 | tf_op jit(solution)/shard_map/ppermute | solution.py:143
  146.9 9.2 %collective-permute-start.11 = (bf16[128,1024]{0,1:T(8,128)(2,1)S(1)}, bf16[128,1024]{0,1:T(8,128)(2,1)S(1)}, u32[]{:S(2)}, u32[]{:S(2)}) collective-permute-start(bf16[128,1024]{0,1:T(8,128)(2,1)S(1)} %collective-permute-done.9), channel_id=1, source_target_pairs={{4,8},{8,12},{12,14},{14,10},{10,6},{6,2},{2,0},{0,4},{5,9},{9,13}... | collective-permute-start | bytes 786440 | tf_op jit(solution)/shard_map/ppermute | solution.py:140
  149.0 0.7 copy-start.7
  150.4 6.8 %collective-permute-start.12 = (bf16[128,1024]{0,1:T(8,128)(2,1)}, bf16[128,1024]{0,1:T(8,128)(2,1)S(1)}, u32[]{:S(2)}, u32[]{:S(2)}) collective-permute-start(bf16[128,1024]{0,1:T(8,128)(2,1)} %copy-done.7), channel_id=1, source_target_pairs={{8,4},{12,8},{14,12},{10,14},{6,10},{2,6},{0,2},{4,0},{9,5},{13,9}... | collective-permute-start | bytes 786440 | tf_op jit(solution)/shard_map/ppermute | solution.py:143
  156.1 6.4 %collective-permute-start.13 = (bf16[128,1024]{0,1:T(8,128)(2,1)S(1)}, bf16[128,1024]{0,1:T(8,128)(2,1)S(1)}, u32[]{:S(2)}, u32[]{:S(2)}) collective-permute-start(bf16[128,1024]{0,1:T(8,128)(2,1)S(1)} %collective-permute-done.11), channel_id=1, source_target_pairs={{4,8},{8,12},{12,14},{14,10},{10,6},{6,2},{2,0},{0,4},{5,9},{9,13}... | collective-permute-start | bytes 786440 | tf_op jit(solution)/shard_map/ppermute | solution.py:140
where the time goes:
time: 165 us; the launch traced here: 164 us
  waiting for transfers between devices  49.3 us (30%)
  local copies, waits for them, and re-layouts  30.2 us (18%)
  other arithmetic  27.9 us (17%)
  starting transfers between devices  27.7 us (17%)
  matrix products  16.9 us (10%)
  between operations  11.7 us (7%)
    ppermute x14, waiting for transfers between devices, gather_blocks(): received.append(lax.ppermute(block, axis, pairs))  29 us
    ppermute x14, starting transfers between devices, gather_blocks(): received.append(lax.ppermute(block, axis, pairs))  16.8 us
    another operation x3, other arithmetic, invert(): factor = jnp.linalg.cholesky(matrix)  12.4 us
    another operation x2, other arithmetic, invert(): lax.linalg.triangular_solve(factor, identity, left_side=True, lower=True)  10.5 us
    all_to_all x1, waiting for transfers between devices, per_device(): expression_genes = lax.all_to_all(sent, 'cell', 1, 0, tiled=True)  9.38 us
    unnamed x32, local copies, waits for them, and re-layouts  8.62 us
    dot_general x26, matrix products, matmul(): return jnp.dot(left, right, precision=lax.Precision.HIGHEST)  8.15 us
    ppermute x4, waiting for transfers between devices, per_device(): ahead = lax.ppermute(ahead, 'cell', forward)  7.9 us
  transfers between devices with their start and end apart: 23, of which 15 were waited for; matrix products, arithmetic and copies ran while one was open for 36% of the time, Pallas kernels for 0%

commit v1 on v0

--- a/solution.py
+++ b/solution.py
@@ -100,7 +100,15 @@
     identity = jnp.eye(width, dtype=jnp.float32)
     design_all = gather_blocks(design, "cell").reshape(-1, width)
     sent = expression + (design_all[0, 0] * 0).astype(expression.dtype)
-    expression_genes = lax.all_to_all(sent, "cell", 1, 0, tiled=True)
+    expression_genes = jnp.concatenate(
+        lax.all_to_all(
+            jnp.stack(jnp.split(sent, lax.axis_size("cell"), axis=1), axis=0),
+            axis_name="cell",
+            concat_axis=0,
+            split_axis=0,
+        ),
+        axis=0,
+    )
     gram_total = lax.dot_general(
         design_all, design_all, (((0,), (0,)), ((), ())), preferred_element_type=jnp.float32
     )

time: 165 us -> 144 us (0.87)
  waiting for transfers between devices: 49.3 us -> 22.9 us
  starting transfers between devices: 27.7 us -> 33.2 us
  matrix products: 16.9 us -> 19.9 us
  other arithmetic: 27.9 us -> 26 us
    ppermute x14, waiting for transfers between devices: 29 us -> 11.3 us  [gather_blocks(): received.append(lax.ppermute(block, axis, pairs))]
    unnamed x32 -> x60, local copies, waits for them, and re-layouts: 8.62 us -> 20.7 us
    all_to_all x2 -> x0, local copies, waits for them, and re-layouts: 7.81 us -> none  [per_device(): expression_genes = lax.all_to_all(sent, 'cell', 1, 0, tiled=True)]
    all_to_all x1, waiting for transfers between devices: 9.38 us -> 1.64 us  [per_device(): lax.all_to_all(jnp.stack(jnp.split(sent, lax.axis_size('cell'), axis=1),...]
    dynamic_update_slice x8, local copies, waits for them, and re-layouts: 5.77 us -> 0.19 us  [place(): return lax.dynamic_update_slice_in_dim(out, piece, start, axis=1)]
    ppermute x14, starting transfers between devices: 16.8 us -> 20.5 us  [gather_blocks(): received.append(lax.ppermute(block, axis, pairs))]
    dot_general x8, matrix products: 4.78 us -> 7.74 us  [place(): fitted = jnp.dot(design, block, preferred_element_type=jnp.float32)]
    ppermute x4, starting transfers between devices: 1.28 us -> 3.62 us  [per_device(): ahead = lax.ppermute(ahead, 'cell', forward)]
  transfers between devices with their start and end apart: 23 -> 23, of which waited for: 15 -> 13; matrix products, arithmetic and copies ran while one was open for 36% -> 41% of each run, Pallas kernels for 0% -> 0%
where the time goes in v1:
time: 144 us; the launch traced here: 143 us
  starting transfers between devices  33.2 us (23%)
  local copies, waits for them, and re-layouts  29.3 us (20%)
  other arithmetic  26 us (18%)
  waiting for transfers between devices  22.9 us (16%)
  matrix products  19.9 us (14%)
  between operations  11.5 us (8%)
    unnamed x60, local copies, waits for them, and re-layouts  20.7 us
    ppermute x14, starting transfers between devices, gather_blocks(): received.append(lax.ppermute(block, axis, pairs))  20.5 us
    another operation x3, other arithmetic, invert(): factor = jnp.linalg.cholesky(matrix)  12.4 us
    ppermute x14, waiting for transfers between devices, gather_blocks(): received.append(lax.ppermute(block, axis, pairs))  11.3 us
    another operation x2, other arithmetic, invert(): lax.linalg.triangular_solve(factor, identity, left_side=True, lower=True)  10.5 us
    dot_general x26, matrix products, matmul(): return jnp.dot(left, right, precision=lax.Precision.HIGHEST)  8.15 us
    dot_general x8, matrix products, place(): fitted = jnp.dot(design, block, preferred_element_type=jnp.float32)  7.74 us
    ppermute x4, waiting for transfers between devices, per_device(): ahead = lax.ppermute(ahead, 'cell', forward)  7.18 us
  transfers between devices with their start and end apart: 23, of which 13 were waited for; matrix products, arithmetic and copies ran while one was open for 41% of the time, Pallas kernels for 0%

profile of v1, /device:TPU:0, one launch (start us, length us, event | category | flops | bytes accessed | tf_op | source)
XLA Modules:
  0.0 142.9 jit_solution(13843700617807546983)
XLA Ops:
  0.6 3.0 %collective-permute-start = (bf16[128,128]{1,0:T(8,128)(2,1)}, bf16[128,128]{1,0:T(8,128)(2,1)S(1)}, u32[]{:S(2)}, u32[]{:S(2)}) collective-permute-start(bf16[128,128]{1,0:T(8,128)(2,1)} %param.6), channel_id=1, source_target_pairs={{0,2},{2,4},{4,6},{6,8},{8,10},{10,12},{12,14},{14,0},{1,3},{3,5},... | collective-permute-start | bytes 98312 | tf_op jit(solution)/shard_map/ppermute | solution.py:79
  3.6 1.6 %collective-permute-start.1 = (bf16[128,128]{1,0:T(8,128)(2,1)}, bf16[128,128]{1,0:T(8,128)(2,1)S(1)}, u32[]{:S(2)}, u32[]{:S(2)}) collective-permute-start(bf16[128,128]{1,0:T(8,128)(2,1)} %param.6), channel_id=1, source_target_pairs={{0,4},{2,6},{4,8},{6,10},{8,12},{10,14},{12,0},{14,2},{1,5},{3,7},... | collective-permute-start | bytes 98312 | tf_op jit(solution)/shard_map/ppermute | solution.py:79
  5.2 2.6 %collective-permute-start.2 = (bf16[128,128]{1,0:T(8,128)(2,1)}, bf16[128,128]{1,0:T(8,128)(2,1)S(1)}, u32[]{:S(2)}, u32[]{:S(2)}) collective-permute-start(bf16[128,128]{1,0:T(8,128)(2,1)} %param.6), channel_id=1, source_target_pairs={{0,6},{2,8},{4,10},{6,12},{8,14},{10,0},{12,2},{14,4},{1,7},{3,9},... | collective-permute-start | bytes 98312 | tf_op jit(solution)/shard_map/ppermute | solution.py:79
  7.8 1.2 collective-permute-start.3
  9.0 2.6 %collective-permute-start.4 = (bf16[128,128]{1,0:T(8,128)(2,1)}, bf16[128,128]{1,0:T(8,128)(2,1)S(1)}, u32[]{:S(2)}, u32[]{:S(2)}) collective-permute-start(bf16[128,128]{1,0:T(8,128)(2,1)} %param.6), channel_id=1, source_target_pairs={{0,10},{2,12},{4,14},{6,0},{8,2},{10,4},{12,6},{14,8},{1,11},{3,13... | collective-permute-start | bytes 98312 | tf_op jit(solution)/shard_map/ppermute | solution.py:79
  11.6 0.8 constant_dynamic-update-slice_fusion.7
  13.1 1.3 collective-permute-start.5
  14.4 1.5 %collective-permute-start.6 = (bf16[128,128]{1,0:T(8,128)(2,1)}, bf16[128,128]{1,0:T(8,128)(2,1)S(1)}, u32[]{:S(2)}, u32[]{:S(2)}) collective-permute-start(bf16[128,128]{1,0:T(8,128)(2,1)} %param.6), channel_id=1, source_target_pairs={{0,14},{2,0},{4,2},{6,4},{8,6},{10,8},{12,10},{14,12},{1,15},{3,1}... | collective-permute-start | bytes 98312 | tf_op jit(solution)/shard_map/ppermute | solution.py:79
  16.0 1.2 collective-permute-done.5
  17.2 1.4 collective-permute-done.6
  21.1 1.7 %broadcast_add_fusion = bf16[128,8192]{1,0:T(8,128)(2,1)S(1)} fusion(bf16[128,8192]{1,0:T(8,128)(2,1)} %param.5, bf16[]{:T(256)} %bitcast.11), kind=kLoop, calls=%fused_computation.38 | loop fusion | flops 1048576 | bytes 4194306 | tf_op jit(solution)/shard_map/add | solution.py:102
  22.8 0.7 fusion.24
  23.6 0.7 fusion.23
  24.3 0.7 fusion.22
  25.0 0.7 fusion.21
  25.7 0.7 fusion.20
  26.4 0.7 fusion.19
  27.2 0.7 fusion.18
  27.9 0.7 fusion.17
  28.6 5.5 %all-to-all-start = ((bf16[8,128,1024]{2,1,0:T(8,128)(2,1)}), bf16[8,128,1024]{2,1,0:T(8,128)(2,1)}, u32[]{:S(2)}, u32[]{:S(2)}) async-start(bf16[8,128,1024]{2,1,0:T(8,128)(2,1)} %fusion.17), calls=%async_computation | async-start | bytes 4194304 | tf_op jit(solution)/shard_map/all_to_all | solution.py:104
  44.3 1.0 constant_dynamic-slice_fusion
  45.3 1.9 %copy.30 = bf16[128,1024]{0,1:T(8,128)(2,1)} copy(bf16[128,1024]{1,0:T(8,128)(2,1)} %get-tuple-element.23) | data formatting | bytes 524288
  47.2 1.8 %copy.29 = bf16[128,1024]{0,1:T(8,128)(2,1)} copy(bf16[128,1024]{1,0:T(8,128)(2,1)} %get-tuple-element.24) | data formatting | bytes 524288
  49.0 1.8 %copy.28 = bf16[128,1024]{0,1:T(8,128)(2,1)} copy(bf16[128,1024]{1,0:T(8,128)(2,1)} %get-tuple-element.25) | data formatting | bytes 524288
  50.8 0.8 copy.27
  51.8 0.8 copy.31
  52.6 0.8 copy.32
  53.5 0.9 copy.33
  54.8 11.7 %cholesky.29 = f32[128,128]{1,0:T(8,128)S(1)} custom-call(f32[128,128]{1,0:T(8,128)S(1)} %fusion.30), custom_call_target="Cholesky" | custom-call | tf_op jit(solution)/shard_map/jit(cholesky)/cholesky | solution.py:18
  67.9 9.8 %custom-call.6 = f32[1,128,128]{1,2,0:T(8,128)S(1)} custom-call(f32[1,128,128]{2,1,0:T(8,128)S(1)} %fusion.26), custom_call_target="InvertDiagBlocksLowerTriangular" | custom-call | tf_op jit(solution)/shard_map/triangular_solve | solution.py:19
  78.2 1.6 %all-to-all-done = bf16[8,128,1024]{2,1,0:T(8,128)(2,1)} async-done(((bf16[8,128,1024]{2,1,0:T(8,128)(2,1)}), bf16[8,128,1024]{2,1,0:T(8,128)(2,1)}, u32[]{:S(2)}, u32[]{:S(2)}) %all-to-all-start) | async-done | bytes 2097184 | tf_op jit(solution)/shard_map/all_to_all | solution.py:104
  79.9 2.4 %convolution_bitcast_fusion.8 = f32[1024,128]{1,0:T(8,128)S(1)} fusion(bf16[8,128,1024]{2,1,0:T(8,128)(2,1)} %all-to-all-done, bf16[8,128,128]{2,1,0:T(8,128)(2,1)S(1)} %copy-done.3, pred[8]{0:T(512)(128)(4,1)S(1)} %compare_and_fusion), kind=kOutput, calls=%fused_computation.18 | convolution fusion | flops 268566528 | bytes 2883592 | tf_op jit(solution)/shard_map/dot_general | solution.py:116
  82.9 1.0 fusion.41
  83.9 1.3 collective-permute-start.8
  85.2 0.8 collective-permute-start.7
  86.5 0.7 collective-permute-done.14
  87.9 1.2 collective-permute-start.15
  90.0 2.4 %collective-permute-start.17 = (f32[128,128]{1,0:T(8,128)S(1)}, f32[128,128]{1,0:T(8,128)S(1)}, u32[]{:S(2)}, u32[]{:S(2)}) collective-permute-start(f32[128,128]{1,0:T(8,128)S(1)} %get-tuple-element.3), channel_id=1, source_target_pairs={{0,6},{2,8},{4,10},{6,12},{8,14},{10,0},{12,2},{14,4},{1,7},{3,9},... | collective-permute-start | bytes 196616 | tf_op jit(solution)/shard_map/ppermute | solution.py:79
  92.4 3.9 %collective-permute-done.15 = f32[128,128]{1,0:T(8,128)S(1)} collective-permute-done((f32[128,128]{1,0:T(8,128)S(1)}, f32[128,128]{1,0:T(8,128)S(1)}, u32[]{:S(2)}, u32[]{:S(2)}) %collective-permute-start.15) | collective-permute-done | bytes 65568 | tf_op jit(solution)/shard_map/ppermute | solution.py:79
  97.5 3.7 %collective-permute-done.17 = f32[128,128]{1,0:T(8,128)S(1)} collective-permute-done((f32[128,128]{1,0:T(8,128)S(1)}, f32[128,128]{1,0:T(8,128)S(1)}, u32[]{:S(2)}, u32[]{:S(2)}) %collective-permute-start.17) | collective-permute-done | bytes 65568 | tf_op jit(solution)/shard_map/ppermute | solution.py:79
  101.3 1.1 collective-permute-start.20
  103.0 1.2 collective-permute-start.21
  106.4 0.9 collective-permute-done.21
  107.9 1.6 %gather_fusion.1 = f32[8,128,128]{2,1,0:T(8,128)S(1)} fusion(f32[8,128,128]{2,1,0:T(8,128)} %bitcast_dynamic-update-slice_fusion, s32[1024]{0:T(1024)S(1)} %pad_clamp_fusion), kind=kCustom, calls=%fused_computation.1 | custom fusion | bytes 1048608 | tf_op jit(solution)/shard_map/jit(_take)/gather | solution.py:81
  110.3 0.8 fusion.16
  111.1 0.8 fusion.32
  116.4 1.4 fusion.8
  117.8 0.9 collective-permute-start.9
  118.7 1.3 subtract_convert_fusion.6
  120.1 1.3 subtract_convert_fusion.5
  121.7 1.2 collective-permute-start.10
  123.0 1.9 %collective-permute-done.9 = bf16[128,1024]{0,1:T(8,128)(2,1)} collective-permute-done((bf16[128,1024]{0,1:T(8,128)(2,1)}, bf16[128,1024]{0,1:T(8,128)(2,1)}, u32[]{:S(2)}, u32[]{:S(2)}) %collective-permute-start.9) | collective-permute-done | bytes 262176 | tf_op jit(solution)/shard_map/ppermute | solution.py:148
  124.9 1.1 collective-permute-start.11
  126.0 1.3 subtract_convert_fusion.4
  127.3 1.1 collective-permute-done.10
  128.4 0.7 copy-done.14
  129.7 1.2 collective-permute-start.12
  131.0 2.3 %collective-permute-done.11 = bf16[128,1024]{0,1:T(8,128)(2,1)} collective-permute-done((bf16[128,1024]{0,1:T(8,128)(2,1)}, bf16[128,1024]{0,1:T(8,128)(2,1)}, u32[]{:S(2)}, u32[]{:S(2)}) %collective-permute-start.11) | collective-permute-done | bytes 262176 | tf_op jit(solution)/shard_map/ppermute | solution.py:148
  133.3 0.8 collective-permute-start.13
  134.1 1.3 subtract_convert_fusion.2
  135.4 0.9 collective-permute-done.12
  137.1 3.0 %collective-permute-done.13 = bf16[128,1024]{0,1:T(8,128)(2,1)} collective-permute-done((bf16[128,1024]{0,1:T(8,128)(2,1)}, bf16[128,1024]{0,1:T(8,128)(2,1)}, u32[]{:S(2)}, u32[]{:S(2)}) %collective-permute-start.13) | collective-permute-done | bytes 262176 | tf_op jit(solution)/shard_map/ppermute | solution.py:148
  140.1 1.3 subtract_convert_fusion
  141.6 1.3 copy-done.1
  (124 shorter events, 19.9 us)
Async XLA Ops:
  0.6 12.4 %collective-permute-start = (bf16[128,128]{1,0:T(8,128)(2,1)}, bf16[128,128]{1,0:T(8,128)(2,1)S(1)}, u32[]{:S(2)}, u32[]{:S(2)}) collective-permute-start(bf16[128,128]{1,0:T(8,128)(2,1)} %param.6), channel_id=1, source_target_pairs={{0,2},{2,4},{4,6},{6,8},{8,10},{10,12},{12,14},{14,0},{1,3},{3,5},... | collective-permute-start | bytes 98312 | tf_op jit(solution)/shard_map/ppermute | solution.py:79
  3.6 10.8 %collective-permute-start.1 = (bf16[128,128]{1,0:T(8,128)(2,1)}, bf16[128,128]{1,0:T(8,128)(2,1)S(1)}, u32[]{:S(2)}, u32[]{:S(2)}) collective-permute-start(bf16[128,128]{1,0:T(8,128)(2,1)} %param.6), channel_id=1, source_target_pairs={{0,4},{2,6},{4,8},{6,10},{8,12},{10,14},{12,0},{14,2},{1,5},{3,7},... | collective-permute-start | bytes 98312 | tf_op jit(solution)/shard_map/ppermute | solution.py:79
  5.2 10.7 %collective-permute-start.2 = (bf16[128,128]{1,0:T(8,128)(2,1)}, bf16[128,128]{1,0:T(8,128)(2,1)S(1)}, u32[]{:S(2)}, u32[]{:S(2)}) collective-permute-start(bf16[128,128]{1,0:T(8,128)(2,1)} %param.6), channel_id=1, source_target_pairs={{0,6},{2,8},{4,10},{6,12},{8,14},{10,0},{12,2},{14,4},{1,7},{3,9},... | collective-permute-start | bytes 98312 | tf_op jit(solution)/shard_map/ppermute | solution.py:79
  7.8 8.2 %collective-permute-start.3 = (bf16[128,128]{1,0:T(8,128)(2,1)}, bf16[128,128]{1,0:T(8,128)(2,1)S(1)}, u32[]{:S(2)}, u32[]{:S(2)}) collective-permute-start(bf16[128,128]{1,0:T(8,128)(2,1)} %param.6), channel_id=1, source_target_pairs={{0,8},{2,10},{4,12},{6,14},{8,0},{10,2},{12,4},{14,6},{1,9},{3,11}... | collective-permute-start | bytes 98312 | tf_op jit(solution)/shard_map/ppermute | solution.py:79
  9.0 6.9 %collective-permute-start.4 = (bf16[128,128]{1,0:T(8,128)(2,1)}, bf16[128,128]{1,0:T(8,128)(2,1)S(1)}, u32[]{:S(2)}, u32[]{:S(2)}) collective-permute-start(bf16[128,128]{1,0:T(8,128)(2,1)} %param.6), channel_id=1, source_target_pairs={{0,10},{2,12},{4,14},{6,0},{8,2},{10,4},{12,6},{14,8},{1,11},{3,13... | collective-permute-start | bytes 98312 | tf_op jit(solution)/shard_map/ppermute | solution.py:79
  13.1 4.1 %collective-permute-start.5 = (bf16[128,128]{1,0:T(8,128)(2,1)}, bf16[128,128]{1,0:T(8,128)(2,1)S(1)}, u32[]{:S(2)}, u32[]{:S(2)}) collective-permute-start(bf16[128,128]{1,0:T(8,128)(2,1)} %param.6), channel_id=1, source_target_pairs={{0,12},{2,14},{4,0},{6,2},{8,4},{10,6},{12,8},{14,10},{1,13},{3,15... | collective-permute-start | bytes 98312 | tf_op jit(solution)/shard_map/ppermute | solution.py:79
  14.4 4.2 %collective-permute-start.6 = (bf16[128,128]{1,0:T(8,128)(2,1)}, bf16[128,128]{1,0:T(8,128)(2,1)S(1)}, u32[]{:S(2)}, u32[]{:S(2)}) collective-permute-start(bf16[128,128]{1,0:T(8,128)(2,1)} %param.6), channel_id=1, source_target_pairs={{0,14},{2,0},{4,2},{6,4},{8,6},{10,8},{12,10},{14,12},{1,15},{3,1}... | collective-permute-start | bytes 98312 | tf_op jit(solution)/shard_map/ppermute | solution.py:79
  19.2 3.6 %copy-start.2 = (bf16[8,128,128]{2,1,0:T(8,128)(2,1)}, bf16[8,128,128]{2,1,0:T(8,128)(2,1)S(1)}, u32[]{:S(2)}) copy-start(bf16[8,128,128]{2,1,0:T(8,128)(2,1)S(1)} %gather_fusion) | copy-start | bytes 786436
  28.6 5.5 %copy-start.15 = (s32[8]{0:T(128)S(1)}, s32[8]{0:T(128)}, u32[]{:S(2)}) copy-start(s32[8]{0:T(128)} %constant.188.clone) | copy-start | bytes 100
  28.6 10.8 %copy-start.13 = (s32[8]{0:T(128)S(1)}, s32[8]{0:T(128)}, u32[]{:S(2)}) copy-start(s32[8]{0:T(128)} %constant.187.clone) | copy-start | bytes 100
  28.6 15.7 %copy-start = (bf16[128,8192]{1,0:T(8,128)(2,1)S(1)}, bf16[128,8192]{1,0:T(8,128)(2,1)}, u32[]{:S(2)}) copy-start(bf16[128,8192]{1,0:T(8,128)(2,1)} %param.5) | copy-start | bytes 6291460
  28.6 51.3 %all-to-all-start = ((bf16[8,128,1024]{2,1,0:T(8,128)(2,1)}), bf16[8,128,1024]{2,1,0:T(8,128)(2,1)}, u32[]{:S(2)}, u32[]{:S(2)}) async-start(bf16[8,128,1024]{2,1,0:T(8,128)(2,1)} %fusion.17), calls=%async_computation | async-start | bytes 4194304 | tf_op jit(solution)/shard_map/all_to_all | solution.py:104
  45.3 9.0 %copy-start.12 = (f32[8192]{0:T(1024)S(1)}, f32[8192]{0:T(1024)}, u32[]{:S(2)}) copy-start(f32[8192]{0:T(1024)} %param.7) | copy-start | bytes 98308
  45.3 9.0 %copy-start.3 = (bf16[8,128,128]{2,1,0:T(8,128)(2,1)S(1)}, bf16[8,128,128]{2,1,0:T(8,128)(2,1)}, u32[]{:S(2)}) copy-start(bf16[8,128,128]{2,1,0:T(8,128)(2,1)} %copy-done.2) | copy-start | bytes 786436
  82.3 3.7 %copy-start.11 = (bf16[128,128]{1,0:T(8,128)(2,1)S(1)}, bf16[128,128]{1,0:T(8,128)(2,1)}, u32[]{:S(2)}) copy-start(bf16[128,128]{1,0:T(8,128)(2,1)} %param.6) | copy-start | bytes 98308
  83.9 36.1 %collective-permute-start.8 = (bf16[128,1024]{0,1:T(8,128)(2,1)S(1)}, bf16[128,1024]{0,1:T(8,128)(2,1)}, u32[]{:S(2)}, u32[]{:S(2)}) collective-permute-start(bf16[128,1024]{0,1:T(8,128)(2,1)S(1)} %convert_bitcast_fusion), channel_id=1, source_target_pairs={{8,4},{12,8},{14,12},{10,14},{6,10},{2,6},{0,2},{4,0},{9,5},{13,9}... | collective-permute-start | bytes 786440 | tf_op jit(solution)/shard_map/ppermute | solution.py:151
  85.2 32.6 %collective-permute-start.7 = (bf16[128,1024]{0,1:T(8,128)(2,1)S(1)}, bf16[128,1024]{0,1:T(8,128)(2,1)}, u32[]{:S(2)}, u32[]{:S(2)}) collective-permute-start(bf16[128,1024]{0,1:T(8,128)(2,1)S(1)} %convert_bitcast_fusion), channel_id=1, source_target_pairs={{4,8},{8,12},{12,14},{14,10},{10,6},{6,2},{2,0},{0,4},{5,9},{9,13}... | collective-permute-start | bytes 786440 | tf_op jit(solution)/shard_map/ppermute | solution.py:148
  86.0 1.3 collective-permute-start.14
  87.9 8.4 %collective-permute-start.15 = (f32[128,128]{1,0:T(8,128)S(1)}, f32[128,128]{1,0:T(8,128)S(1)}, u32[]{:S(2)}, u32[]{:S(2)}) collective-permute-start(f32[128,128]{1,0:T(8,128)S(1)} %get-tuple-element.3), channel_id=1, source_target_pairs={{0,2},{2,4},{4,6},{6,8},{8,10},{10,12},{12,14},{14,0},{1,3},{3,5},... | collective-permute-start | bytes 196616 | tf_op jit(solution)/shard_map/ppermute | solution.py:79
  89.4 7.5 %collective-permute-start.16 = (f32[128,128]{1,0:T(8,128)S(1)}, f32[128,128]{1,0:T(8,128)S(1)}, u32[]{:S(2)}, u32[]{:S(2)}) collective-permute-start(f32[128,128]{1,0:T(8,128)S(1)} %get-tuple-element.3), channel_id=1, source_target_pairs={{0,4},{2,6},{4,8},{6,10},{8,12},{10,14},{12,0},{14,2},{1,5},{3,7},... | collective-permute-start | bytes 196616 | tf_op jit(solution)/shard_map/ppermute | solution.py:79
  90.0 11.2 %collective-permute-start.17 = (f32[128,128]{1,0:T(8,128)S(1)}, f32[128,128]{1,0:T(8,128)S(1)}, u32[]{:S(2)}, u32[]{:S(2)}) collective-permute-start(f32[128,128]{1,0:T(8,128)S(1)} %get-tuple-element.3), channel_id=1, source_target_pairs={{0,6},{2,8},{4,10},{6,12},{8,14},{10,0},{12,2},{14,4},{1,7},{3,9},... | collective-permute-start | bytes 196616 | tf_op jit(solution)/shard_map/ppermute | solution.py:79
  96.3 6.7 %collective-permute-start.18 = (f32[128,128]{1,0:T(8,128)S(1)}, f32[128,128]{1,0:T(8,128)S(1)}, u32[]{:S(2)}, u32[]{:S(2)}) collective-permute-start(f32[128,128]{1,0:T(8,128)S(1)} %get-tuple-element.3), channel_id=1, source_target_pairs={{0,8},{2,10},{4,12},{6,14},{8,0},{10,2},{12,4},{14,6},{1,9},{3,11}... | collective-permute-start | bytes 196616 | tf_op jit(solution)/shard_map/ppermute | solution.py:79
  96.9 8.0 %collective-permute-start.19 = (f32[128,128]{1,0:T(8,128)S(1)}, f32[128,128]{1,0:T(8,128)S(1)}, u32[]{:S(2)}, u32[]{:S(2)}) collective-permute-start(f32[128,128]{1,0:T(8,128)S(1)} %get-tuple-element.3), channel_id=1, source_target_pairs={{0,10},{2,12},{4,14},{6,0},{8,2},{10,4},{12,6},{14,8},{1,11},{3,13... | collective-permute-start | bytes 196616 | tf_op jit(solution)/shard_map/ppermute | solution.py:79
  101.3 4.5 %collective-permute-start.20 = (f32[128,128]{1,0:T(8,128)S(1)}, f32[128,128]{1,0:T(8,128)S(1)}, u32[]{:S(2)}, u32[]{:S(2)}) collective-permute-start(f32[128,128]{1,0:T(8,128)S(1)} %get-tuple-element.3), channel_id=1, source_target_pairs={{0,12},{2,14},{4,0},{6,2},{8,4},{10,6},{12,8},{14,10},{1,13},{3,15... | collective-permute-start | bytes 196616 | tf_op jit(solution)/shard_map/ppermute | solution.py:79
  103.0 4.3 %collective-permute-start.21 = (f32[128,128]{1,0:T(8,128)S(1)}, f32[128,128]{1,0:T(8,128)S(1)}, u32[]{:S(2)}, u32[]{:S(2)}) collective-permute-start(f32[128,128]{1,0:T(8,128)S(1)} %get-tuple-element.3), channel_id=1, source_target_pairs={{0,14},{2,0},{4,2},{6,4},{8,6},{10,8},{12,10},{14,12},{1,15},{3,1}... | collective-permute-start | bytes 196616 | tf_op jit(solution)/shard_map/ppermute | solution.py:79
  113.0 5.7 %copy-start.10 = (bf16[128,1024]{0,1:T(8,128)(2,1)S(1)}, bf16[128,1024]{0,1:T(8,128)(2,1)}, u32[]{:S(2)}) copy-start(bf16[128,1024]{0,1:T(8,128)(2,1)} %copy.27) | copy-start | bytes 786436
  114.1 6.0 %copy-start.9 = (bf16[128,1024]{0,1:T(8,128)(2,1)S(1)}, bf16[128,1024]{0,1:T(8,128)(2,1)}, u32[]{:S(2)}) copy-start(bf16[128,1024]{0,1:T(8,128)(2,1)} %copy.28) | copy-start | bytes 786436
  117.8 8.2 %copy-start.8 = (bf16[128,1024]{0,1:T(8,128)(2,1)S(1)}, bf16[128,1024]{0,1:T(8,128)(2,1)}, u32[]{:S(2)}) copy-start(bf16[128,1024]{0,1:T(8,128)(2,1)} %copy.29) | copy-start | bytes 786436
  117.8 7.1 %collective-permute-start.9 = (bf16[128,1024]{0,1:T(8,128)(2,1)}, bf16[128,1024]{0,1:T(8,128)(2,1)}, u32[]{:S(2)}, u32[]{:S(2)}) collective-permute-start(bf16[128,1024]{0,1:T(8,128)(2,1)} %collective-permute-done.7), channel_id=1, source_target_pairs={{4,8},{8,12},{12,14},{14,10},{10,6},{6,2},{2,0},{0,4},{5,9},{9,13}... | collective-permute-start | bytes 786440 | tf_op jit(solution)/shard_map/ppermute | solution.py:148
  120.0 9.0 %copy-start.7 = (bf16[128,1024]{0,1:T(8,128)(2,1)S(1)}, bf16[128,1024]{0,1:T(8,128)(2,1)}, u32[]{:S(2)}) copy-start(bf16[128,1024]{0,1:T(8,128)(2,1)} %copy.30) | copy-start | bytes 786436
  121.7 6.6 %collective-permute-start.10 = (bf16[128,1024]{0,1:T(8,128)(2,1)}, bf16[128,1024]{0,1:T(8,128)(2,1)S(1)}, u32[]{:S(2)}, u32[]{:S(2)}) collective-permute-start(bf16[128,1024]{0,1:T(8,128)(2,1)} %collective-permute-done.8), channel_id=1, source_target_pairs={{8,4},{12,8},{14,12},{10,14},{6,10},{2,6},{0,2},{4,0},{9,5},{13,9}... | collective-permute-start | bytes 786440 | tf_op jit(solution)/shard_map/ppermute | solution.py:151
  123.0 11.1 %copy-start.6 = (bf16[128,1024]{0,1:T(8,128)(2,1)S(1)}, bf16[128,1024]{0,1:T(8,128)(2,1)}, u32[]{:S(2)}) copy-start(bf16[128,1024]{0,1:T(8,128)(2,1)} %copy.31) | copy-start | bytes 786436
  124.9 8.4 %collective-permute-start.11 = (bf16[128,1024]{0,1:T(8,128)(2,1)}, bf16[128,1024]{0,1:T(8,128)(2,1)}, u32[]{:S(2)}, u32[]{:S(2)}) collective-permute-start(bf16[128,1024]{0,1:T(8,128)(2,1)} %collective-permute-done.9), channel_id=1, source_target_pairs={{4,8},{8,12},{12,14},{14,10},{10,6},{6,2},{2,0},{0,4},{5,9},{9,13}... | collective-permute-start | bytes 786440 | tf_op jit(solution)/shard_map/ppermute | solution.py:148
  127.3 9.1 %copy-start.5 = (bf16[128,1024]{0,1:T(8,128)(2,1)S(1)}, bf16[128,1024]{0,1:T(8,128)(2,1)}, u32[]{:S(2)}) copy-start(bf16[128,1024]{0,1:T(8,128)(2,1)} %copy.32) | copy-start | bytes 786436
  128.4 0.7 copy-start.14
  129.7 6.6 %collective-permute-start.12 = (bf16[128,1024]{0,1:T(8,128)(2,1)}, bf16[128,1024]{0,1:T(8,128)(2,1)S(1)}, u32[]{:S(2)}, u32[]{:S(2)}) collective-permute-start(bf16[128,1024]{0,1:T(8,128)(2,1)} %copy-done.14), channel_id=1, source_target_pairs={{8,4},{12,8},{14,12},{10,14},{6,10},{2,6},{0,2},{4,0},{9,5},{13,9}... | collective-permute-start | bytes 786440 | tf_op jit(solution)/shard_map/ppermute | solution.py:151
  131.0 9.1 %copy-start.4 = (bf16[128,1024]{0,1:T(8,128)(2,1)S(1)}, bf16[128,1024]{0,1:T(8,128)(2,1)}, u32[]{:S(2)}) copy-start(bf16[128,1024]{0,1:T(8,128)(2,1)} %copy.33) | copy-start | bytes 786436
  133.3 6.8 %collective-permute-start.13 = (bf16[128,1024]{0,1:T(8,128)(2,1)}, bf16[128,1024]{0,1:T(8,128)(2,1)}, u32[]{:S(2)}, u32[]{:S(2)}) collective-permute-start(bf16[128,1024]{0,1:T(8,128)(2,1)} %collective-permute-done.11), channel_id=1, source_target_pairs={{4,8},{8,12},{12,14},{14,10},{10,6},{6,2},{2,0},{0,4},{5,9},{9,13}... | collective-permute-start | bytes 786440 | tf_op jit(solution)/shard_map/ppermute | solution.py:148
  141.6 1.3 copy-start.1
